TPU v7x, 256 devices: a whole 4x4x8 slice. The times are simulated.
256 devices in a mesh: cfg: 2 (over core), req: 8 (over z), seq: 16 (over y, x).
Axes of the slice: x: 4, y: 4, z: 8, core: 2. Of those that a mesh axis runs over, the one named last changes fastest.
Arguments:
- img_hidden: bfloat16 [2, 16, 512, 1536], P('cfg', 'req', 'seq'), may hold values from -6 to 6
- txt_hidden: bfloat16 [2, 16, 160, 1536], P('cfg', 'req', 'seq'), may hold values from -6 to 6
- text_len: int32 [2, 16], P('cfg'), may hold values from 1 to 154, as said below
- pooled: float32 [2, 16, 1536], P('cfg'), may hold values from -6 to 6
- timestep: int32 [16], replicated, may hold values from 0 to 27
- latent: float32 [16, 512, 64], P('req', 'seq', 'cfg'), may hold values from -24 to 24
- mod_weight: bfloat16 [1536, 15360], P(None, ('req', 'seq')), may hold values from -0.15625 to 0.15625
- mod_bias: float32 [15360], P(('req', 'seq')), may hold values from -2 to 2
- img_qkv: bfloat16 [1536, 3, 1536], P(None, None, 'req'), may hold values from -2.5 to 2.5
- txt_kv: bfloat16 [1536, 2, 1536], P(None, None, 'req'), may hold values from -0.15625 to 0.15625
- out_weight: bfloat16 [1536, 1536], P('req'), may hold values from -0.15625 to 0.15625
- fc_in: bfloat16 [1536, 6144], P(None, 'seq'), may hold values from -0.15625 to 0.15625
- fc_out: bfloat16 [6144, 1536], P('seq'), may hold values from -0.078125 to 0.078125
- final_weight: bfloat16 [1536, 64], replicated, may hold values from -0.15625 to 0.15625
Outputs:
- velocity: float32 [16, 512, 64], P('req', 'seq', 'cfg')
- next_latent: float32 [16, 512, 64], P('req', 'seq', 'cfg')
- latent_norm: float32 [16], P('req')
- latent_peak: float32 [16], P('req')
Inputs may be any that keep to these rules, and one draw needn't show every extreme that they name: Text slots from text_len to 159 of a request are padding; every draw has a request of length 154 and one of length 1.
All inputs are finite; a program needn't handle non-finite values.
Results may differ from a plain program's by a relative error of at most 0.015.
Values may be sent and summed in bfloat16 or wider, within the bound.
No kernel may reach another device: no remote copies, remote signals or barrier semaphores. Data moves between devices by JAX's collectives and lax.ppermute only.
A program may use at most 64 MiB of HBM per device.

v0:
```python
import math
import jax
import jax.numpy as jnp
from jax import lax
from jax.sharding import PartitionSpec as P

D = 1536
HD = 64
PATCHC = 64
IMG = 512
STEPS = 28
SIGMA_SHIFT = 3.0
GUIDANCE = 5.0
EPSILON = 1e-06
MASKED_SCORE = -1e30


def from_partner(value, axis, distance):
    mask = 2**distance
    pairs = [(source, source ^ mask) for source in range(lax.axis_size(axis))]
    return lax.ppermute(value, axis, pairs)


def shifted(fraction):
    return SIGMA_SHIFT * fraction / (1.0 + (SIGMA_SHIFT - 1.0) * fraction)


def plan(timestep):
    position = timestep.astype(jnp.float32)
    return (shifted(1.0 - position / STEPS), shifted(1.0 - (position + 1.0) / STEPS))


def time_features(sigma):
    half_width = D // 2
    frequency = jnp.exp(-math.log(10000.0) * jnp.arange(half_width, dtype=jnp.float32) / half_width)
    angles = (1000.0 * sigma)[:, None] * frequency[None, :]
    return jnp.concatenate([jnp.cos(angles), jnp.sin(angles)], axis=1)


def layer_norm(values):
    average = jnp.mean(values, axis=-1, keepdims=True)
    centred = values - average
    spread = jnp.mean(centred * centred, axis=-1, keepdims=True)
    return centred * lax.rsqrt(spread + EPSILON)


def attention(queries, key_rows, value_rows, live_keys):
    query_count = queries.shape[0]
    head_count = queries.shape[1]
    block_rows = min(512, query_count)
    scale_factor = HD ** (-0.5)

    def one_block(query_block):
        scores = (
            jnp.einsum("qhd,khd->hqk", query_block, key_rows, preferred_element_type=jnp.float32)
            * scale_factor
        )
        scores = jnp.where(live_keys[None, None, :], scores, MASKED_SCORE)
        highest = jnp.max(scores, axis=-1, keepdims=True)
        exp_scores = jnp.exp(scores - highest)
        weights = (exp_scores / jnp.sum(exp_scores, axis=-1, keepdims=True)).astype(jnp.bfloat16)
        mixture = jnp.einsum(
            "hqk,khd->qhd", weights, value_rows, preferred_element_type=jnp.float32
        )
        return mixture.astype(jnp.bfloat16)

    blocks = queries.reshape(query_count // block_rows, block_rows, head_count, HD)
    return lax.map(one_block, blocks).reshape(query_count, head_count * HD)


def on_device(
    img_hidden,
    txt_hidden,
    text_len,
    pooled,
    timestep,
    latent,
    mod_weight,
    mod_bias,
    img_qkv,
    txt_kv,
    out_weight,
    fc_in,
    fc_out,
    final_weight,
):
    group_size = img_hidden.shape[1]
    current, upcoming = plan(timestep)
    activated = jax.nn.silu(pooled[0] + time_features(current)).astype(jnp.bfloat16)
    columns = jnp.dot(activated, mod_weight, preferred_element_type=jnp.float32) + mod_bias
    every_mod = lax.all_gather(columns, ("req", "seq"), axis=1, tiled=True)
    offset = lax.axis_index("req") * group_size
    modulation = lax.dynamic_slice_in_dim(every_mod, offset, group_size, 0).reshape(
        group_size, 10, 1, D
    )
    shift_attn, scale_attn, gate_attn = (modulation[:, 0], modulation[:, 1], modulation[:, 2])
    shift_mlp, scale_mlp, gate_mlp = (modulation[:, 3], modulation[:, 4], modulation[:, 5])
    shift_text, scale_text = (modulation[:, 6], modulation[:, 7])
    scale_final, shift_final = (modulation[:, 8], modulation[:, 9])
    img_float = img_hidden[0].astype(jnp.float32)
    img_in = (layer_norm(img_float) * (1.0 + scale_attn) + shift_attn).astype(jnp.bfloat16)
    txt_in = (
        layer_norm(txt_hidden[0].astype(jnp.float32)) * (1.0 + scale_text) + shift_text
    ).astype(jnp.bfloat16)
    all_img, all_txt = (
        lax.all_gather(img_in, "req", axis=0, tiled=True),
        lax.all_gather(txt_in, "req", axis=0, tiled=True),
    )
    head_width = img_qkv.shape[2]
    local_heads = head_width // HD
    qkv_columns = img_qkv.reshape(D, 3 * head_width)
    kv_columns = txt_kv.reshape(D, 2 * head_width)
    own_img, own_txt = (
        lax.all_to_all(all_img, "seq", split_axis=0, concat_axis=1, tiled=True),
        lax.all_to_all(all_txt, "seq", split_axis=0, concat_axis=1, tiled=True),
    )
    own_proj = jnp.einsum(
        "rnd,dc->rnc", own_img, qkv_columns, preferred_element_type=jnp.float32
    ).astype(jnp.bfloat16)
    own_proj_txt = jnp.einsum(
        "rnd,dc->rnc", own_txt, kv_columns, preferred_element_type=jnp.float32
    ).astype(jnp.bfloat16)
    local_count = own_proj.shape[0]
    image_rows = own_proj.shape[1]
    text_rows = own_proj_txt.shape[1]
    first_request = lax.axis_index("seq") * local_count

    def attend_request(operands):
        projected, projected_txt, request_slot = operands
        queries = projected[:, :head_width]
        key_rows = jnp.concatenate(
            [projected[:, head_width : 2 * head_width], projected_txt[:, :head_width]], axis=0
        )
        value_rows = jnp.concatenate(
            [projected[:, 2 * head_width :], projected_txt[:, head_width:]], axis=0
        )
        text_count = lax.dynamic_index_in_dim(text_len[0], first_request + request_slot, 0, False)
        live_keys = jnp.arange(image_rows + text_rows, dtype=jnp.int32) < image_rows + text_count
        total_keys = image_rows + text_rows
        return attention(
            queries.reshape(image_rows, local_heads, HD),
            key_rows.reshape(total_keys, local_heads, HD),
            value_rows.reshape(total_keys, local_heads, HD),
            live_keys,
        )

    attended = lax.map(
        attend_request, (own_proj, own_proj_txt, jnp.arange(local_count, dtype=jnp.int32))
    )
    projected_rows = jnp.einsum(
        "rnk,kd->rnd", attended, out_weight, preferred_element_type=jnp.float32
    )
    moved_rows = lax.all_to_all(
        projected_rows.astype(jnp.bfloat16), "seq", split_axis=1, concat_axis=0, tiled=True
    ).astype(projected_rows.dtype)
    attn_out = lax.psum_scatter(
        moved_rows.astype(jnp.bfloat16), "req", scatter_dimension=0, tiled=True
    ).astype(jnp.float32)
    img_mid = img_float + gate_attn * attn_out
    mlp_in = (layer_norm(img_mid) * (1.0 + scale_mlp) + shift_mlp).astype(jnp.bfloat16)
    raised = jnp.einsum(
        "rnd,df->rnf",
        lax.all_gather(mlp_in, "seq", axis=1, tiled=True),
        fc_in,
        preferred_element_type=jnp.float32,
    )
    hidden = jax.nn.gelu(raised, approximate=True).astype(jnp.bfloat16)
    mlp_terms = jnp.einsum("rnf,fd->rnd", hidden, fc_out, preferred_element_type=jnp.float32)
    mlp_out = lax.psum_scatter(
        mlp_terms.astype(jnp.bfloat16), "seq", scatter_dimension=1, tiled=True
    ).astype(jnp.float32)
    img_out = img_mid + gate_mlp * mlp_out
    final_in = (layer_norm(img_out) * (1.0 + scale_final) + shift_final).astype(jnp.bfloat16)
    own_velocity = jnp.einsum(
        "rnd,dc->rnc", final_in, final_weight, preferred_element_type=jnp.float32
    )
    half_values = latent.shape[2]
    half_index = lax.axis_index("cfg")
    kept_velocity = lax.dynamic_slice_in_dim(own_velocity, half_index * half_values, half_values, 2)
    sent_velocity = lax.dynamic_slice_in_dim(
        own_velocity, (1 - half_index) * half_values, half_values, 2
    )
    other_velocity = from_partner(sent_velocity, "cfg", 0)
    cond_first = half_index == 0
    conditional = jnp.where(cond_first, kept_velocity, other_velocity)
    unconditional = jnp.where(cond_first, other_velocity, kept_velocity)
    guided = unconditional + GUIDANCE * (conditional - unconditional)
    step_size = lax.dynamic_slice_in_dim(upcoming - current, offset, group_size, 0)
    next_latent = latent + step_size[:, None, None] * guided
    squares = jnp.sum(next_latent * next_latent, axis=(1, 2))
    largest = jnp.max(jnp.abs(next_latent), axis=(1, 2))
    square_total = lax.psum(squares, ("cfg", "seq"))
    peak_value = lax.pmax(largest, ("cfg", "seq"))
    latent_norm = jnp.sqrt(square_total / (IMG * PATCHC))
    return (guided, next_latent, latent_norm, peak_value)


def solution(mesh):
    placed = (
        P("cfg", "req", "seq", None),
        P("cfg", "req", "seq", None),
        P("cfg", None),
        P("cfg", None, None),
        P(),
        P("req", "seq", "cfg"),
        P(None, ("req", "seq")),
        P(("req", "seq")),
        P(None, None, "req"),
        P(None, None, "req"),
        P("req", None),
        P(None, "seq"),
        P("seq", None),
        P(),
    )
    return jax.shard_map(
        on_device,
        mesh=mesh,
        in_specs=placed,
        out_specs=(P("req", "seq", "cfg"), P("req", "seq", "cfg"), P("req"), P("req")),
        check_vma=False,
    )
```

profile of v0, /device:TPU:1, one launch (start us, length us, event | category | flops | bytes accessed | tf_op | source)
XLA Modules:
  0.0 808.6 jit_solution(5461950614559532431)
XLA Ops:
  9.5 299.6 %all-gather = f32[128,120,16]{1,2,0:T(8,128)S(1)} all-gather(f32[1,120,16]{1,2,0:T(8,128)S(1)} %fusion.18), channel_id=1, replica_groups=mesh['cfg'=2,'req'=8,'seq'=16] {'req','seq'}, dimensions={0}, use_global_device_ids=true | all-gather | bytes 990720 | tf_op jit(solution)/shard_map/all_gather | solution.py:91
  314.5 19.9 %all_gather.14 = bf16[16,10,1536]{2,1,0:T(8,128)(2,1)S(1)} all-gather(bf16[2,10,1536]{2,1,0:T(8,128)(2,1)S(1)} %fusion.42), channel_id=1, replica_groups=mesh['cfg'=2,'req'=8,'seq'=16] {'req'}, dimensions={0}, use_global_device_ids=true | all-gather | bytes 552960 | tf_op jit(solution)/shard_map/all_gather | solution.py:107
  334.4 13.0 %all_to_all.30 = bf16[16,10,1536]{2,1,0:T(8,128)(2,1)S(1)} all-to-all(bf16[16,10,1536]{2,1,0:T(8,128)(2,1)S(1)} %all_gather.14), channel_id=1, replica_groups=mesh['cfg'=2,'req'=8,'seq'=16] {'seq'}, dimensions={0} | all-to-all | bytes 983040 | tf_op jit(solution)/shard_map/all_to_all | solution.py:115
  347.4 51.1 %all-gather.4.cloned.1.call-done = bf16[16,32,1536]{2,1,0:T(8,128)(2,1)} async-done(((bf16[2,32,1536]{2,1,0:T(8,128)(2,1)}), bf16[16,32,1536]{2,1,0:T(8,128)(2,1)}) %all-gather.4.cloned.1.call-update) | async-done | bytes 1572880 | tf_op jit(solution)/shard_map/all_gather | solution.py:106
  398.5 5.8 all-to-all-start
  406.0 1.7 convolution_convert_fusion.3
  407.8 13.1 %all-to-all-done = bf16[16,32,1536]{2,1,0:T(8,128)(2,1)} async-done(((bf16[16,32,1536]{2,1,0:T(8,128)(2,1)}), bf16[16,32,1536]{2,1,0:T(8,128)(2,1)}, u32[]{:S(2)}, u32[]{:S(2)}) %all-to-all-start) | async-done | bytes 1572896 | tf_op jit(solution)/shard_map/all_to_all | solution.py:114
  420.9 2.5 convolution_convert_fusion.2
  423.5 3.5 fusion.63
  427.1 2.7 fusion.17
  430.4 4.1 copy.58
  435.0 11.5 %reduce.2 = bf16[512,1536]{1,0:T(8,128)(2,1)S(1)} reduce(bf16[512,1,1536]{2,1,0:T(2,128)(2,1)} %bitcast.126, bf16[]{:T(256)} %broadcast.203), dimensions={1}, to_apply=%bitcast.124.reduce_sub_computation | reduce | bytes 3145730
  446.5 2.1 reshape.184
  448.6 18.4 %all_to_all.31 = bf16[16,2,24576]{2,1,0:T(2,128)(2,1)S(1)} all-to-all(bf16[16,2,24576]{2,1,0:T(2,128)(2,1)} %reshape.184), channel_id=1, replica_groups=mesh['cfg'=2,'req'=8,'seq'=16] {'seq'}, dimensions={0} | all-to-all | bytes 3145728 | tf_op jit(solution)/shard_map/all_to_all | solution.py:153
  466.9 6.3 reshape.185
  473.2 3.4 copy.36
  477.3 42.2 %reduce-scatter.3.cloned.1.call-done = bf16[2,32,1536]{2,1,0:T(8,128)(2,1)} async-done(((bf16[16,32,1536]{2,1,0:T(8,128)(2,1)}), bf16[2,32,1536]{2,1,0:T(8,128)(2,1)}) %reduce-scatter.3.cloned.1.call-update) | async-done | bytes 196624 | tf_op jit(solution)/shard_map/reduce_scatter | solution.py:156
  521.7 1.8 add_convert_fusion.1
  523.5 54.8 %all-gather.6.cloned.1.call-done = bf16[2,512,1536]{2,1,0:T(8,128)(2,1)} async-done(((bf16[2,32,1536]{2,1,0:T(8,128)(2,1)}), bf16[2,512,1536]{2,1,0:T(8,128)(2,1)}) %all-gather.6.cloned.1.call-update) | async-done | bytes 3145744 | tf_op jit(solution)/shard_map/all_gather | solution.py:163
  578.4 7.6 convolution_convert_fusion
  586.6 78.8 %reduce-scatter.5.cloned.1.call-done = bf16[2,32,1536]{2,1,0:T(8,128)(2,1)} async-done(((bf16[2,512,1536]{2,1,0:T(8,128)(2,1)}), bf16[2,32,1536]{2,1,0:T(8,128)(2,1)}) %reduce-scatter.5.cloned.1.call-update) | async-done | bytes 196624 | tf_op jit(solution)/shard_map/reduce_scatter | solution.py:169
  669.1 2.4 collective-permute-start
  673.1 65.3 %psum.7 = f32[2]{0:T(128)S(1)} all-reduce(f32[2]{0:T(128)S(1)} %get-tuple-element.41), channel_id=1, replica_groups=mesh['cfg'=2,'req'=8,'seq'=16] {'cfg','seq'}, use_global_device_ids=true, to_apply=%region_13.14 | all-reduce | flops 2 | bytes 16 | tf_op jit(solution)/shard_map/psum | solution.py:192
  738.8 63.2 %pmax.7 = f32[2]{0:T(128)} all-reduce(f32[2]{0:T(128)S(1)} %get-tuple-element.40), channel_id=1, replica_groups=mesh['cfg'=2,'req'=8,'seq'=16] {'cfg','seq'}, use_global_device_ids=true, to_apply=%region_15.16 | all-reduce | flops 2 | bytes 16 | tf_op jit(solution)/shard_map/pmax | solution.py:193
  (85 shorter events, 19.9 us)
Async XLA Ops:
  7.2 413.7 %copy-start = (bf16[1536,3,192]{0,2,1:T(8,128)(2,1)S(1)}, bf16[1536,3,192]{0,2,1:T(8,128)(2,1)}, u32[]{:S(2)}) copy-start(bf16[1536,3,192]{0,2,1:T(8,128)(2,1)} %param.22) | copy-start | bytes 5308420
  7.2 391.3 %all-gather.4.cloned.1.call-start = ((), (), s32[]{:S(2)}) async-start(), calls=%async_computation.5 | async-start | bytes 1769472 | tf_op jit(solution)/shard_map/all_gather | solution.py:106
  309.4 3.5 copy-start.1
  309.4 4.7 copy-start.4
  347.4 57.1 %copy-start.13 = (s32[1,16]{1,0:T(1,128)S(1)}, s32[1,16]{1,0:T(1,128)}, u32[]{:S(2)}) copy-start(s32[1,16]{1,0:T(1,128)} %param.16) | copy-start | bytes 196
  398.5 22.4 %all-to-all-start = ((bf16[16,32,1536]{2,1,0:T(8,128)(2,1)}), bf16[16,32,1536]{2,1,0:T(8,128)(2,1)}, u32[]{:S(2)}, u32[]{:S(2)}) async-start(bf16[16,32,1536]{2,1,0:T(8,128)(2,1)} %all-gather.4.cloned.1.call-done), calls=%async_computation | async-start | bytes 3145728 | tf_op jit(solution)/shard_map/all_to_all | solution.py:114
  404.3 115.1 %reduce-scatter.3.cloned.1.call-start = ((), (), s32[]{:S(2)}) async-start(), calls=%async_computation.6 | async-start | bytes 1769472 | tf_op jit(solution)/shard_map/reduce_scatter | solution.py:156
  427.1 2.7 copy-start.3
  476.5 0.7 copy-start.5
  476.5 0.7 copy-start.8
  476.5 0.7 copy-start.9
  476.5 101.8 %copy-start.11 = (bf16[384,1536]{1,0:T(8,128)(2,1)S(1)}, bf16[384,1536]{1,0:T(8,128)(2,1)}, u32[]{:S(2)}) copy-start(bf16[384,1536]{1,0:T(8,128)(2,1)} %param.26) | copy-start | bytes 3538948
  476.6 101.8 %all-gather.6.cloned.1.call-start = ((), (), s32[]{:S(2)}) async-start(), calls=%async_computation.7 | async-start | bytes 3342336 | tf_op jit(solution)/shard_map/all_gather | solution.py:163
  523.5 142.0 %reduce-scatter.5.cloned.1.call-start = ((), (), s32[]{:S(2)}) async-start(), calls=%async_computation.8 | async-start | bytes 3342336 | tf_op jit(solution)/shard_map/reduce_scatter | solution.py:169
  585.9 0.7 copy-start.6
  585.9 0.7 copy-start.7
  585.9 79.6 %copy-start.2 = (bf16[2,32,1536]{2,1,0:T(8,128)(2,1)S(1)}, bf16[2,32,1536]{2,1,0:T(8,128)(2,1)}, u32[]{:S(2)}) copy-start(bf16[2,32,1536]{2,1,0:T(8,128)(2,1)} %reduce-scatter.3.cloned.1.call-done) | copy-start | bytes 589828
  585.9 81.9 %copy-start.12 = (bf16[1536,64]{0,1:T(8,128)(2,1)S(1)}, bf16[1536,64]{0,1:T(8,128)(2,1)}, u32[]{:S(2)}) copy-start(bf16[1536,64]{0,1:T(8,128)(2,1)} %param.27) | copy-start | bytes 589828
  585.9 86.4 %copy-start.10 = (f32[2,32,32]{2,1,0:T(8,128)S(1)}, f32[2,32,32]{2,1,0:T(8,128)}, u32[]{:S(2)}) copy-start(f32[2,32,32]{2,1,0:T(8,128)} %param.19) | copy-start | bytes 24580
  669.1 3.3 collective-permute-start
Sparse Core Ops, SparseCore 0:
  314.2 84.2 all-gather.3
  476.7 42.7 reduce-scatter.2
  523.6 54.7 all-gather.5
  586.1 79.3 reduce-scatter.4
where the time goes:
time: 809 us
  blocking collectives  479 us (59%)
  waiting for transfers between devices  241 us (30%)
  other arithmetic  23.5 us (3%)
  local copies, waits for them, and re-layouts  21.2 us (3%)
  matrix products  21.1 us (3%)
  between operations  14 us (2%)
  starting transfers between devices  8.55 us (1%)
    all_gather x1, blocking collectives, on_device(): every_mod = lax.all_gather(columns, ('req', 'seq'), axis=1, tiled=True)  300 us
    reduce_scatter x1, waiting for transfers between devices, on_device(): lax.psum_scatter(mlp_terms.astype(jnp.bfloat16), 'seq', scatter_dimension...  78.8 us
    psum x1, blocking collectives, on_device(): square_total = lax.psum(squares, ('cfg', 'seq'))  65.3 us
    pmax x1, blocking collectives, on_device(): peak_value = lax.pmax(largest, ('cfg', 'seq'))  63.2 us
    all_gather x1, waiting for transfers between devices, on_device(): lax.all_gather(mlp_in, 'seq', axis=1, tiled=True)  54.8 us
    all_gather x1, waiting for transfers between devices, on_device(): lax.all_gather(img_in, 'req', axis=0, tiled=True)  51.1 us
    reduce_scatter x1, waiting for transfers between devices, on_device(): lax.psum_scatter(moved_rows.astype(jnp.bfloat16), 'req', scatter_dimensio...  42.2 us
    all_gather x1, blocking collectives, on_device(): lax.all_gather(txt_in, 'req', axis=0, tiled=True)  19.9 us
  transfers between devices with their start and end apart: 6, of which 6 were waited for; matrix products, arithmetic and copies ran while one was open for 0% of the time, Pallas kernels for 0%

commit v1 on v0

--- a/solution.py
+++ b/solution.py
@@ -189,7 +189,7 @@
     next_latent = latent + step_size[:, None, None] * guided
     squares = jnp.sum(next_latent * next_latent, axis=(1, 2))
     largest = jnp.max(jnp.abs(next_latent), axis=(1, 2))
-    square_total = lax.psum(squares, ("cfg", "seq"))
+    square_total = lax.all_gather(squares, ("cfg", "seq")).sum(axis=0)
     peak_value = lax.pmax(largest, ("cfg", "seq"))
     latent_norm = jnp.sqrt(square_total / (IMG * PATCHC))
     return (guided, next_latent, latent_norm, peak_value)

time: 809 us -> 810 us (level)
    psum x1 -> x0, blocking collectives: 65.3 us -> none  [on_device(): square_total = lax.psum(squares, ('cfg', 'seq'))]
    unnamed x0 -> x1, blocking collectives: none -> 65 us
  transfers between devices with their start and end apart: 6 -> 6, of which waited for: 6 -> 5; matrix products, arithmetic and copies ran while one was open for 0% -> 1% of each run, Pallas kernels for 0% -> 0%
where the time goes in v1:
time: 810 us; the launch traced here: 809 us
  blocking collectives  479 us (59%)
  waiting for transfers between devices  240 us (30%)
  other arithmetic  23.6 us (3%)
  local copies, waits for them, and re-layouts  22 us (3%)
  matrix products  21.1 us (3%)
  between operations  14.7 us (2%)
  starting transfers between devices  8.55 us (1%)
    all_gather x1, blocking collectives, on_device(): every_mod = lax.all_gather(columns, ('req', 'seq'), axis=1, tiled=True)  300 us
    reduce_scatter x1, waiting for transfers between devices, on_device(): lax.psum_scatter(mlp_terms.astype(jnp.bfloat16), 'seq', scatter_dimension...  78.8 us
    unnamed x1, blocking collectives  65 us
    pmax x1, blocking collectives, on_device(): peak_value = lax.pmax(largest, ('cfg', 'seq'))  63.4 us
    all_gather x1, waiting for transfers between devices, on_device(): lax.all_gather(mlp_in, 'seq', axis=1, tiled=True)  54.8 us
    all_gather x1, waiting for transfers between devices, on_device(): lax.all_gather(img_in, 'req', axis=0, tiled=True)  51.1 us
    reduce_scatter x1, waiting for transfers between devices, on_device(): lax.psum_scatter(moved_rows.astype(jnp.bfloat16), 'req', scatter_dimensio...  42.2 us
    all_gather x1, blocking collectives, on_device(): lax.all_gather(txt_in, 'req', axis=0, tiled=True)  19.9 us
  transfers between devices with their start and end apart: 6, of which 5 were waited for; matrix products, arithmetic and copies ran while one was open for 1% of the time, Pallas kernels for 0%

profile of v1, /device:TPU:1, one launch (start us, length us, event | category | flops | bytes accessed | tf_op | source)
XLA Modules:
  0.0 809.3 jit_solution(5338575640614300922)
XLA Ops:
  9.5 299.6 %all-gather.1 = f32[128,120,16]{1,2,0:T(8,128)S(1)} all-gather(f32[1,120,16]{1,2,0:T(8,128)S(1)} %fusion.18), channel_id=1, replica_groups=mesh['cfg'=2,'req'=8,'seq'=16] {'req','seq'}, dimensions={0}, use_global_device_ids=true | all-gather | bytes 990720 | tf_op jit(solution)/shard_map/all_gather | solution.py:91
  314.5 19.9 %all_gather.20 = bf16[16,10,1536]{2,1,0:T(8,128)(2,1)S(1)} all-gather(bf16[2,10,1536]{2,1,0:T(8,128)(2,1)S(1)} %fusion.42), channel_id=1, replica_groups=mesh['cfg'=2,'req'=8,'seq'=16] {'req'}, dimensions={0}, use_global_device_ids=true | all-gather | bytes 552960 | tf_op jit(solution)/shard_map/all_gather | solution.py:107
  334.4 13.0 %all_to_all.30 = bf16[16,10,1536]{2,1,0:T(8,128)(2,1)S(1)} all-to-all(bf16[16,10,1536]{2,1,0:T(8,128)(2,1)S(1)} %all_gather.20), channel_id=1, replica_groups=mesh['cfg'=2,'req'=8,'seq'=16] {'seq'}, dimensions={0} | all-to-all | bytes 983040 | tf_op jit(solution)/shard_map/all_to_all | solution.py:115
  347.4 51.1 %all-gather.5.cloned.1.call-done = bf16[16,32,1536]{2,1,0:T(8,128)(2,1)} async-done(((bf16[2,32,1536]{2,1,0:T(8,128)(2,1)}), bf16[16,32,1536]{2,1,0:T(8,128)(2,1)}) %all-gather.5.cloned.1.call-update) | async-done | bytes 1572880 | tf_op jit(solution)/shard_map/all_gather | solution.py:106
  398.5 5.8 all-to-all-start
  406.0 1.7 convolution_convert_fusion.3
  407.8 13.1 %all-to-all-done = bf16[16,32,1536]{2,1,0:T(8,128)(2,1)} async-done(((bf16[16,32,1536]{2,1,0:T(8,128)(2,1)}), bf16[16,32,1536]{2,1,0:T(8,128)(2,1)}, u32[]{:S(2)}, u32[]{:S(2)}) %all-to-all-start) | async-done | bytes 1572896 | tf_op jit(solution)/shard_map/all_to_all | solution.py:114
  420.9 2.5 convolution_convert_fusion.2
  423.5 3.5 fusion.63
  427.1 2.7 fusion.17
  430.4 4.1 copy.58
  435.0 11.5 %reduce.2 = bf16[512,1536]{1,0:T(8,128)(2,1)S(1)} reduce(bf16[512,1,1536]{2,1,0:T(2,128)(2,1)} %bitcast.127, bf16[]{:T(256)} %broadcast.204), dimensions={1}, to_apply=%bitcast.125.reduce_sub_computation | reduce | bytes 3145730
  446.5 2.1 reshape.190
  448.6 18.4 %all_to_all.31 = bf16[16,2,24576]{2,1,0:T(2,128)(2,1)S(1)} all-to-all(bf16[16,2,24576]{2,1,0:T(2,128)(2,1)} %reshape.190), channel_id=1, replica_groups=mesh['cfg'=2,'req'=8,'seq'=16] {'seq'}, dimensions={0} | all-to-all | bytes 3145728 | tf_op jit(solution)/shard_map/all_to_all | solution.py:153
  466.9 6.3 reshape.191
  473.2 3.4 copy.36
  477.3 42.2 %reduce-scatter.3.cloned.1.call-done = bf16[2,32,1536]{2,1,0:T(8,128)(2,1)} async-done(((bf16[16,32,1536]{2,1,0:T(8,128)(2,1)}), bf16[2,32,1536]{2,1,0:T(8,128)(2,1)}) %reduce-scatter.3.cloned.1.call-update) | async-done | bytes 196624 | tf_op jit(solution)/shard_map/reduce_scatter | solution.py:156
  521.7 1.8 add_convert_fusion.1
  523.5 54.8 %all-gather.7.cloned.1.call-done = bf16[2,512,1536]{2,1,0:T(8,128)(2,1)} async-done(((bf16[2,32,1536]{2,1,0:T(8,128)(2,1)}), bf16[2,512,1536]{2,1,0:T(8,128)(2,1)}) %all-gather.7.cloned.1.call-update) | async-done | bytes 3145744 | tf_op jit(solution)/shard_map/all_gather | solution.py:163
  578.4 7.6 convolution_convert_fusion
  586.6 78.8 %reduce-scatter.5.cloned.1.call-done = bf16[2,32,1536]{2,1,0:T(8,128)(2,1)} async-done(((bf16[2,512,1536]{2,1,0:T(8,128)(2,1)}), bf16[2,32,1536]{2,1,0:T(8,128)(2,1)}) %reduce-scatter.5.cloned.1.call-update) | async-done | bytes 196624 | tf_op jit(solution)/shard_map/reduce_scatter | solution.py:169
  669.1 2.4 collective-permute-start
  673.7 65.0 %all-reduce = f32[64]{0:T(128)S(1)} all-reduce(f32[64]{0:T(128)S(1)} %dynamic-update-slice), channel_id=2, replica_groups=mesh['cfg'=2,'req'=8,'seq'=16] {'cfg','seq'}, use_global_device_ids=true, to_apply=%add | all-reduce | flops 64 | bytes 512
  739.4 63.4 %pmax.7 = f32[2]{0:T(128)} all-reduce(f32[2]{0:T(128)S(1)} %get-tuple-element.40), channel_id=1, replica_groups=mesh['cfg'=2,'req'=8,'seq'=16] {'cfg','seq'}, use_global_device_ids=true, to_apply=%region_15.16 | all-reduce | flops 2 | bytes 16 | tf_op jit(solution)/shard_map/pmax | solution.py:193
  (92 shorter events, 20.1 us)
Async XLA Ops:
  7.2 413.7 %copy-start = (bf16[1536,3,192]{0,2,1:T(8,128)(2,1)S(1)}, bf16[1536,3,192]{0,2,1:T(8,128)(2,1)}, u32[]{:S(2)}) copy-start(bf16[1536,3,192]{0,2,1:T(8,128)(2,1)} %param.22) | copy-start | bytes 5308420
  7.2 391.3 %all-gather.5.cloned.1.call-start = ((), (), s32[]{:S(2)}) async-start(), calls=%async_computation.5 | async-start | bytes 1769472 | tf_op jit(solution)/shard_map/all_gather | solution.py:106
  309.4 3.5 copy-start.1
  309.4 4.7 copy-start.4
  347.4 57.1 %copy-start.13 = (s32[1,16]{1,0:T(1,128)S(1)}, s32[1,16]{1,0:T(1,128)}, u32[]{:S(2)}) copy-start(s32[1,16]{1,0:T(1,128)} %param.16) | copy-start | bytes 196
  398.5 22.4 %all-to-all-start = ((bf16[16,32,1536]{2,1,0:T(8,128)(2,1)}), bf16[16,32,1536]{2,1,0:T(8,128)(2,1)}, u32[]{:S(2)}, u32[]{:S(2)}) async-start(bf16[16,32,1536]{2,1,0:T(8,128)(2,1)} %all-gather.5.cloned.1.call-done), calls=%async_computation | async-start | bytes 3145728 | tf_op jit(solution)/shard_map/all_to_all | solution.py:114
  404.3 115.1 %reduce-scatter.3.cloned.1.call-start = ((), (), s32[]{:S(2)}) async-start(), calls=%async_computation.6 | async-start | bytes 1769472 | tf_op jit(solution)/shard_map/reduce_scatter | solution.py:156
  427.1 2.7 copy-start.3
  476.5 0.7 copy-start.5
  476.5 0.7 copy-start.8
  476.5 0.7 copy-start.9
  476.5 101.8 %copy-start.11 = (bf16[384,1536]{1,0:T(8,128)(2,1)S(1)}, bf16[384,1536]{1,0:T(8,128)(2,1)}, u32[]{:S(2)}) copy-start(bf16[384,1536]{1,0:T(8,128)(2,1)} %param.26) | copy-start | bytes 3538948
  476.6 101.8 %all-gather.7.cloned.1.call-start = ((), (), s32[]{:S(2)}) async-start(), calls=%async_computation.7 | async-start | bytes 3342336 | tf_op jit(solution)/shard_map/all_gather | solution.py:163
  523.5 142.0 %reduce-scatter.5.cloned.1.call-start = ((), (), s32[]{:S(2)}) async-start(), calls=%async_computation.8 | async-start | bytes 3342336 | tf_op jit(solution)/shard_map/reduce_scatter | solution.py:169
  585.9 0.7 copy-start.6
  585.9 0.7 copy-start.7
  585.9 79.6 %copy-start.2 = (bf16[2,32,1536]{2,1,0:T(8,128)(2,1)S(1)}, bf16[2,32,1536]{2,1,0:T(8,128)(2,1)}, u32[]{:S(2)}) copy-start(bf16[2,32,1536]{2,1,0:T(8,128)(2,1)} %reduce-scatter.3.cloned.1.call-done) | copy-start | bytes 589828
  585.9 81.9 %copy-start.12 = (bf16[1536,64]{0,1:T(8,128)(2,1)S(1)}, bf16[1536,64]{0,1:T(8,128)(2,1)}, u32[]{:S(2)}) copy-start(bf16[1536,64]{0,1:T(8,128)(2,1)} %param.27) | copy-start | bytes 589828
  585.9 85.6 %copy-start.14 = (u32[256]{0:T(256)S(1)}, u32[256]{0:T(256)}, u32[]{:S(2)}) copy-start(u32[256]{0:T(256)} %constant.136) | copy-start | bytes 3076
  586.0 86.8 %copy-start.10 = (f32[2,32,32]{2,1,0:T(8,128)S(1)}, f32[2,32,32]{2,1,0:T(8,128)}, u32[]{:S(2)}) copy-start(f32[2,32,32]{2,1,0:T(8,128)} %param.19) | copy-start | bytes 24580
  669.1 3.7 collective-permute-start
Sparse Core Ops, SparseCore 0:
  314.2 84.2 all-gather.4
  476.7 42.7 reduce-scatter.2
  523.6 54.7 all-gather.6
  586.1 79.3 reduce-scatter.4
